TPU v7x, 32 devices: a whole 2x2x4 slice. The times are simulated.
32 devices in a mesh: region: 4 (over z), narrow: 8 (over y, x, core).
Axes of the slice: x: 2, y: 2, z: 4, core: 2. Of those that a mesh axis runs over, the one named last changes fastest.
Arguments:
- dust_pos: float32 [3, 6144], P(None, ('region', 'narrow')), may hold values from -1 to 1
- dust_vel: float32 [3, 6144], P(None, ('region', 'narrow')), may hold values from -6 to 6
- dust_tau: float32 [6144], P(('region', 'narrow')), may hold values from 0.02 to 2
- dest: int32 [6144, 1], P(('region', 'narrow')), may hold values from 0 to 3; in each aligned block of 192 rows (0 to 191, 192 to 383, ...) at most 96 rows name the same one
- counts: int32 [32], P(('region', 'narrow')), may hold values from 96 to 192, as said below
- wake_pos: float32 [3, 32768], P(None, ('region', 'narrow')), may hold values from -1 to 1
- wake_gamma: float32 [3, 32768], P(None, ('region', 'narrow')), may hold values from -0.3 to 0.3
- wake_core: float32 [32768], P(('region', 'narrow')), may hold values from 0.05 to 0.3
Outputs:
- moved: float32 [6, 12288], P(None, ('region', 'narrow'))
Inputs may be any that keep to these rules, and one draw needn't show every extreme that they name: `dest`: in each device's 192 rows, no region is named by more than 96 rows, and some device's rows name some region exactly 96 times. `counts`: some device has all its rows live in every draw.
All inputs are finite; a program needn't handle non-finite values.
Results may differ from a plain program's by a relative error of at most 0.0003.
Values sent between devices are 32-bit elements; how exact they have to be, the bound alone decides.
No kernel may reach another device: no remote copies, remote signals or barrier semaphores. Data moves between devices by JAX's collectives and lax.ppermute only.
A program may use at most 64 MiB of HBM per device.

v0:
```python
import math
import jax
import jax.numpy as jnp
from jax import lax
from jax.sharding import PartitionSpec as P

step_size = 0.1
gravity = 1.0


def cross_rows(first, second):
    return jnp.stack(
        [
            first[1] * second[2] - first[2] * second[1],
            first[2] * second[0] - first[0] * second[2],
            first[0] * second[1] - first[1] * second[0],
        ]
    )


def raw_terms(points, wake_block):
    point_count = points.shape[1]
    wake_count = wake_block.shape[1]
    wake_width = math.gcd(wake_count, 2048)
    wake_place = wake_block[0:3]
    vortex_gamma = wake_block[3:6]
    core_square = wake_block[6] * wake_block[6]
    tables = jnp.concatenate([vortex_gamma, cross_rows(vortex_gamma, wake_place)], axis=0)
    place_blocks = wake_place.reshape(3, wake_count // wake_width, wake_width).transpose(1, 0, 2)
    table_blocks = tables.reshape(6, wake_count // wake_width, wake_width).transpose(1, 0, 2)
    core_blocks = core_square.reshape(wake_count // wake_width, wake_width)
    point_blocks = points.reshape(3, point_count // point_count, point_count).transpose(1, 0, 2)

    def one_block(point_group):

        def accumulate(running, parts):
            place_part, table_part, core_part = parts
            first_gap = point_group[0][:, None] - place_part[0][None, :]
            second_gap = point_group[1][:, None] - place_part[1][None, :]
            third_gap = point_group[2][:, None] - place_part[2][None, :]
            distance_sq = (
                first_gap * first_gap
                + second_gap * second_gap
                + third_gap * third_gap
                + core_part[None, :]
            )
            inverse_root = lax.rsqrt(distance_sq)
            kernel = inverse_root * inverse_root * inverse_root
            product = lax.dot_general(
                table_part, kernel, (((1,), (1,)), ((), ())), precision=lax.Precision.HIGH
            )
            return (running + product, None)

        total, _ = lax.scan(
            accumulate,
            jnp.zeros((6, point_count), jnp.float32),
            (place_blocks, table_blocks, core_blocks),
        )
        return total

    result = lax.map(one_block, point_blocks)
    return result.transpose(1, 0, 2).reshape(6, point_count)


def advance(arrived, raw_sums):
    points = arrived[0:3]
    velocity = arrived[3:6]
    live_flag = arrived[7]
    wind = (cross_rows(raw_sums[0:3], points) - raw_sums[3:6]) / (4.0 * math.pi)
    safe_tau = jnp.where(live_flag > 0.5, arrived[6], 1.0)
    rate = step_size / safe_tau
    upward = jnp.array([0.0, 0.0, 1.0], jnp.float32)[:, None]
    new_velocity = (velocity + rate[None, :] * wind - step_size * gravity * upward) / (
        1.0 + rate[None, :]
    )
    new_place = points + step_size * new_velocity
    return jnp.concatenate([new_place, new_velocity], axis=0) * live_flag[None, :]


def exchange_slots(outgoing, capacity):
    regions = lax.axis_size("region")
    if regions > 8:
        return lax.all_to_all(outgoing, "region", split_axis=1, concat_axis=1, tiled=True)
    region = lax.axis_index("region")
    blocks = outgoing.reshape(outgoing.shape[0], regions, capacity)
    by_shift = [jnp.take(blocks, region, axis=1)]
    for shift in range(1, regions):
        pairs = [(i, (i + shift) % regions) for i in range(regions)]
        sent = jnp.take(blocks, (region + shift) % regions, axis=1)
        by_shift.append(lax.ppermute(sent, "region", pairs))
    stacked = jnp.stack(by_shift, axis=1)
    order = (region - jnp.arange(regions, dtype=jnp.int32)) % regions
    return jnp.take(stacked, order, axis=1).reshape(outgoing.shape[0], regions * capacity)


def body(dust_pos, dust_vel, dust_tau, dest, counts, wake_pos, wake_gamma, wake_core):
    per_device = dust_tau.shape[0]
    regions = lax.axis_size("region")
    capacity = 2 * per_device // regions
    slot_count = regions * capacity
    live_rows = (jnp.arange(per_device, dtype=jnp.int32) < counts[0]).astype(jnp.float32)
    target = dest[:, 0]
    row = jnp.arange(per_device, dtype=jnp.int32)
    earlier = (target[:, None] == target[None, :]) & (row[None, :] < row[:, None])
    slot_rank = jnp.sum(earlier.astype(jnp.int32), axis=1)
    column = target * capacity + slot_rank
    placing = (column[:, None] == jnp.arange(slot_count, dtype=jnp.int32)[None, :]).astype(
        jnp.float32
    )
    dust_state = (
        jnp.concatenate(
            [dust_pos, dust_vel, dust_tau[None, :], jnp.ones((1, per_device), jnp.float32)], axis=0
        )
        * live_rows[None, :]
    )
    outgoing = jnp.dot(
        dust_state, placing, precision=lax.Precision.HIGHEST, preferred_element_type=jnp.float32
    )
    wake_rows = jnp.concatenate([wake_pos, wake_gamma, wake_core[None, :]], axis=0)
    outgoing, wake_rows = lax.optimization_barrier((outgoing, wake_rows))
    arrived = exchange_slots(outgoing, capacity)
    region_wake = lax.all_gather(wake_rows, "narrow", axis=1, tiled=True)
    points = arrived[0:3]
    raw_sums = raw_terms(points, region_wake)
    return advance(arrived, raw_sums)


def solution(mesh):
    in_specs = (
        P(None, ("region", "narrow")),
        P(None, ("region", "narrow")),
        P(("region", "narrow")),
        P(("region", "narrow"), None),
        P(("region", "narrow")),
        P(None, ("region", "narrow")),
        P(None, ("region", "narrow")),
        P(("region", "narrow")),
    )
    out_specs = P(None, ("region", "narrow"))
    return jax.shard_map(body, mesh=mesh, in_specs=in_specs, out_specs=out_specs, check_vma=False)
```

profile of v0, /device:TPU:0, one launch (start us, length us, event | category | flops | bytes accessed | tf_op | source)
XLA Modules:
  0.0 33.0 jit_solution(9160325887394976063)
XLA Ops:
  0.0 0.9 %convert_reduce_fusion = s32[192]{0:T(256)S(1)} fusion(s32[192]{0:T(256)} %bitcast.62), kind=kLoop, calls=%fused_computation.34 | loop fusion | flops 184128 | bytes 1536 | tf_op jit(solution)/shard_map/reduce_sum | solution.py:105
  0.9 0.7 %multiply_add_fusion.1 = s32[192,1]{0,1:T(1,128)S(1)} fusion(s32[192,1]{0,1:T(1,128)S(1)} %bitcast.65, s32[192,1]{0,1:T(1,128)} %param.16), kind=kLoop, calls=%fused_computation.87 | loop fusion | flops 384 | bytes 2304 | tf_op jit(solution)/shard_map/add | solution.py:106
  2.3 0.1 pad.21.clone
  2.4 0.8 %pad_maximum_fusion = f32[7,1024]{1,0:T(8,128)S(1)} fusion(f32[1,1024]{1,0:T(1,128)} %bitcast.63, f32[3,1024]{1,0:T(4,128)} %param.19, f32[3,1024]{1,0:T(4,128)} %param.18), kind=kLoop, calls=%fused_computation.40 | loop fusion | flops 14336 | bytes 57344 | tf_op jit(solution)/shard_map/concatenate | solution.py:119
  3.1 1.0 %fusion.22 = f32[8,384]{1,0:T(8,128)S(1)} fusion(s32[192]{0:T(256)S(1)} %bitcast.69, f32[1,192]{1,0:T(1,128)} %bitcast.70, f32[3,192]{1,0:T(4,128)} %param.14, f32[3,192]{1,0:T(4,128)} %param.13, f32[8]{0:T(128)S(1)} %pad.21.clone, f32[192]{0:T(256)S(1)} %compare_convert_fusion), kind=kOutput, calls=%fused_computation.32 | convolution fusion | flops 7157760 | bytes 19232 | tf_op jit(solution)/shard_map/dot_general | solution.py:116
  4.1 0.1 reshape.132
  4.3 3.1 %collective-permute-start = (f32[8,96]{1,0:T(8,128)S(1)}, f32[8,96]{1,0:T(8,128)S(1)}, u32[]{:S(2)}, u32[]{:S(2)}) collective-permute-start(f32[8,96]{1,0:T(8,128)S(1)} %select_bitcast_fusion.2), channel_id=1, source_target_pairs={{0,8},{8,16},{16,24},{24,0},{1,9},{9,17},{17,25},{25,1},{2,10},{10... | collective-permute-start | bytes 9224 | tf_op jit(solution)/shard_map/ppermute | solution.py:90
  7.3 2.6 %collective-permute-start.1 = (f32[8,96]{1,0:T(8,128)S(1)}, f32[8,96]{1,0:T(8,128)S(1)}, u32[]{:S(2)}, u32[]{:S(2)}) collective-permute-start(f32[8,96]{1,0:T(8,128)S(1)} %select_bitcast_fusion.1), channel_id=1, source_target_pairs={{0,16},{8,24},{16,0},{24,8},{1,17},{9,25},{17,1},{25,9},{2,18},{10... | collective-permute-start | bytes 9224 | tf_op jit(solution)/shard_map/ppermute | solution.py:90
  9.9 1.3 %collective-permute-start.2 = (f32[8,96]{1,0:T(8,128)S(1)}, f32[8,96]{1,0:T(8,128)S(1)}, u32[]{:S(2)}, u32[]{:S(2)}) collective-permute-start(f32[8,96]{1,0:T(8,128)S(1)} %bitcast.64), channel_id=1, source_target_pairs={{0,24},{8,0},{16,8},{24,16},{1,25},{9,1},{17,9},{25,17},{2,26},{10... | collective-permute-start | bytes 9224 | tf_op jit(solution)/shard_map/ppermute | solution.py:90
  11.3 9.3 %all_gather.3 = f32[7,8192]{1,0:T(8,128)S(1)} all-gather(f32[7,1024]{1,0:T(8,128)S(1)} %pad_maximum_fusion), channel_id=1, replica_groups=mesh['region'=4,'narrow'=8] {'narrow'}, dimensions={1}, use_global_device_ids=true | all-gather | bytes 258048 | tf_op jit(solution)/shard_map/all_gather | solution.py:122
  20.6 0.3 fusion.25
  20.9 0.1 fusion.42
  21.0 0.1 maximum_bitcast_fusion
  21.2 0.6 %gather_fusion = f32[4,8,96]{2,1,0:T(8,128)S(1)} fusion(f32[8,4,96]{2,0,1:T(8,128)S(1)} %pad_maximum_fusion.1, s32[1024]{0:T(1024)S(1)} %pad_clamp_fusion), kind=kCustom, calls=%fused_computation | custom fusion | bytes 24592 | tf_op jit(solution)/shard_map/jit(_take)/gather | solution.py:93
  21.8 0.1 select_bitcast_fusion
  21.9 0.1 slice.122
  22.0 9.7 %while.19 = (s32[]{:T(128)}, f32[6,384]{1,0:T(8,128)S(1)}, f32[4,6,2048]{2,1,0:T(8,128)S(1)}, f32[3,384]{1,0:T(4,128)S(1)}, f32[4,3,2048]{2,1,0:T(4,128)S(1)}, /...) while((s32[]{:T(128)}, f32[6,384]{1,0:T(8,128)S(1)}, ...), condition=%wide.region_2.4_spmd.clone, body=%wide.region_1.0_spmd.clone.sunk | while | flops 36966916 | bytes 200859 | solution.py:54
  22.1 2.3 %fusion.47 = f32[6,384]{1,0:T(8,128)S(1)} fusion(f32[2048]{0:T(1024)S(1)} %bitcast.55, f32[2048]{0:T(1024)S(1)} %bitcast.54, f32[384]{0:T(512)S(1)} %get-tuple-element.179, f32[2048]{0:T(1024)S(1)} %bitcast.53, f32[384]{0:T(512)S(1)} %get-tuple-element.181, f32[2048]{0:T(1024)S(1)} %bitcast.52, f32[384]{0:T(512)S(1)} %get-tuple-element.183, ...), kind=kOutput, calls=%fused_computation.20.clone.1 | convolution fusion | flops 36966912 | bytes 125957 | tf_op jit(solution)/shard_map/while/body/eval_jaxpr/while/body/eval_jaxpr/dot_general | solution.py:49
  24.4 0.1 constant_dynamic-slice_fusion.10
  24.5 2.3 %fusion.47 = f32[6,384]{1,0:T(8,128)S(1)} fusion(f32[2048]{0:T(1024)S(1)} %bitcast.55, f32[2048]{0:T(1024)S(1)} %bitcast.54, f32[384]{0:T(512)S(1)} %get-tuple-element.179, f32[2048]{0:T(1024)S(1)} %bitcast.53, f32[384]{0:T(512)S(1)} %get-tuple-element.181, f32[2048]{0:T(1024)S(1)} %bitcast.52, f32[384]{0:T(512)S(1)} %get-tuple-element.183, ...), kind=kOutput, calls=%fused_computation.20.clone.1 | convolution fusion | flops 36966912 | bytes 125957 | tf_op jit(solution)/shard_map/while/body/eval_jaxpr/while/body/eval_jaxpr/dot_general | solution.py:49
  26.8 0.1 constant_dynamic-slice_fusion.10
  27.0 2.3 %fusion.47 = f32[6,384]{1,0:T(8,128)S(1)} fusion(f32[2048]{0:T(1024)S(1)} %bitcast.55, f32[2048]{0:T(1024)S(1)} %bitcast.54, f32[384]{0:T(512)S(1)} %get-tuple-element.179, f32[2048]{0:T(1024)S(1)} %bitcast.53, f32[384]{0:T(512)S(1)} %get-tuple-element.181, f32[2048]{0:T(1024)S(1)} %bitcast.52, f32[384]{0:T(512)S(1)} %get-tuple-element.183, ...), kind=kOutput, calls=%fused_computation.20.clone.1 | convolution fusion | flops 36966912 | bytes 125957 | tf_op jit(solution)/shard_map/while/body/eval_jaxpr/while/body/eval_jaxpr/dot_general | solution.py:49
  29.3 0.1 constant_dynamic-slice_fusion.10
  29.4 2.3 %fusion.47 = f32[6,384]{1,0:T(8,128)S(1)} fusion(f32[2048]{0:T(1024)S(1)} %bitcast.55, f32[2048]{0:T(1024)S(1)} %bitcast.54, f32[384]{0:T(512)S(1)} %get-tuple-element.179, f32[2048]{0:T(1024)S(1)} %bitcast.53, f32[384]{0:T(512)S(1)} %get-tuple-element.181, f32[2048]{0:T(1024)S(1)} %bitcast.52, f32[384]{0:T(512)S(1)} %get-tuple-element.183, ...), kind=kOutput, calls=%fused_computation.20.clone.1 | convolution fusion | flops 36966912 | bytes 125957 | tf_op jit(solution)/shard_map/while/body/eval_jaxpr/while/body/eval_jaxpr/dot_general | solution.py:49
  31.7 0.1 squeeze.24
  31.8 0.1 squeeze.25
  31.9 0.1 squeeze.26
  32.0 0.1 squeeze.30
  32.1 0.1 squeeze.31
  32.2 0.1 slice.124
  32.3 0.1 multiply_add_fusion
  32.4 0.6 %maximum_multiply_fusion = f32[6,384]{1,0:T(8,128)} fusion(f32[3,384]{1,0:T(4,128)S(1)} %get-tuple-element.114, f32[3,384]{1,0:T(4,128)S(1)} %get-tuple-element.113, f32[384]{0:T(512)S(1)} %squeeze.30), kind=kLoop, calls=%fused_computation.46 | loop fusion | flops 4608 | bytes 19968 | tf_op jit(solution)/shard_map/mul | solution.py:77
  (32 shorter events, 0.4 us)
Async XLA Ops:
  4.3 16.9 %collective-permute-start = (f32[8,96]{1,0:T(8,128)S(1)}, f32[8,96]{1,0:T(8,128)S(1)}, u32[]{:S(2)}, u32[]{:S(2)}) collective-permute-start(f32[8,96]{1,0:T(8,128)S(1)} %select_bitcast_fusion.2), channel_id=1, source_target_pairs={{0,8},{8,16},{16,24},{24,0},{1,9},{9,17},{17,25},{25,1},{2,10},{10... | collective-permute-start | bytes 9224 | tf_op jit(solution)/shard_map/ppermute | solution.py:90
  7.3 13.8 %collective-permute-start.1 = (f32[8,96]{1,0:T(8,128)S(1)}, f32[8,96]{1,0:T(8,128)S(1)}, u32[]{:S(2)}, u32[]{:S(2)}) collective-permute-start(f32[8,96]{1,0:T(8,128)S(1)} %select_bitcast_fusion.1), channel_id=1, source_target_pairs={{0,16},{8,24},{16,0},{24,8},{1,17},{9,25},{17,1},{25,9},{2,18},{10... | collective-permute-start | bytes 9224 | tf_op jit(solution)/shard_map/ppermute | solution.py:90
  9.9 11.2 %collective-permute-start.2 = (f32[8,96]{1,0:T(8,128)S(1)}, f32[8,96]{1,0:T(8,128)S(1)}, u32[]{:S(2)}, u32[]{:S(2)}) collective-permute-start(f32[8,96]{1,0:T(8,128)S(1)} %bitcast.64), channel_id=1, source_target_pairs={{0,24},{8,0},{16,8},{24,16},{1,25},{9,1},{17,9},{25,17},{2,26},{10... | collective-permute-start | bytes 9224 | tf_op jit(solution)/shard_map/ppermute | solution.py:90
  22.0 10.4 %copy-start = (f32[3]{0:T(128)S(1)}, f32[3]{0:T(128)}, u32[]{:S(2)}) copy-start(f32[3]{0:T(128)} %constant.129) | copy-start | bytes 40
where the time goes:
time: 33.5 us; the launch traced here: 33 us
  matrix products  10.2 us (30%)
  blocking collectives  9.32 us (28%)
  starting transfers between devices  7.01 us (21%)
  other arithmetic  3.64 us (11%)
  local copies, waits for them, and re-layouts  1.92 us (6%)
  between operations  0.83 us (2%)
    all_gather x1, blocking collectives, body(): region_wake = lax.all_gather(wake_rows, 'narrow', axis=1, tiled=True)  9.32 us
    dot_general x4, matrix products, accumulate(): lax.dot_general(table_part, kernel, (((1,), (1,)), ((), ())), precision=l...  9.21 us
    ppermute x3, starting transfers between devices, exchange_slots(): by_shift.append(lax.ppermute(sent, 'region', pairs))  7.01 us
    dot_general x1, matrix products, body(): jnp.dot(dust_state, placing, precision=lax.Precision.HIGHEST, preferred_e...  1 us
    reduce_sum x1, other arithmetic, body(): slot_rank = jnp.sum(earlier.astype(jnp.int32), axis=1)  0.93 us
    concatenate x1, other arithmetic, body(): jnp.concatenate([wake_pos, wake_gamma, wake_core[None, :]], axis=0)  0.77 us
    add x1, other arithmetic, body(): column = target * capacity + slot_rank  0.69 us
  transfers between devices with their start and end apart: 3, of which 0 were waited for; matrix products, arithmetic and copies ran while one was open for 2% of the time, Pallas kernels for 0%

commit v1 on v0

--- a/solution.py
+++ b/solution.py
@@ -1,3 +1,4 @@
+import functools
 import math
 import jax
 import jax.numpy as jnp
@@ -6,6 +7,24 @@
 
 step_size = 0.1
 gravity = 1.0
+
+
+def launch_the_screen(inner_x, link_axis, join_dim):
+    series = [inner_x]
+    total_devices = jax.lax.axis_size(link_axis)
+    for c in range(total_devices - 1):
+        taken_in = jax.lax.ppermute(
+            series[-1],
+            axis_name=link_axis,
+            perm=[(m, (m + 1) % total_devices) for m in range(total_devices)],
+        )
+        series.append(taken_in)
+    fresh = jnp.concatenate(series[::-1], join_dim)
+    shaped = jax.lax.axis_index(link_axis)
+    return jnp.roll(fresh, (shaped + 1) * inner_x.shape[join_dim], axis=join_dim)
+
+
+group_the_cubes = functools.partial(launch_the_screen, link_axis="narrow", join_dim=1)
 
 
 def cross_rows(first, second):
@@ -119,7 +138,7 @@
     wake_rows = jnp.concatenate([wake_pos, wake_gamma, wake_core[None, :]], axis=0)
     outgoing, wake_rows = lax.optimization_barrier((outgoing, wake_rows))
     arrived = exchange_slots(outgoing, capacity)
-    region_wake = lax.all_gather(wake_rows, "narrow", axis=1, tiled=True)
+    region_wake = group_the_cubes(wake_rows)
     points = arrived[0:3]
     raw_sums = raw_terms(points, region_wake)
     return advance(arrived, raw_sums)

time: 33.5 us -> 48.9 us (1.46)
  waiting for transfers between devices: 0.01 us -> 23.4 us
  blocking collectives: 9.32 us -> 0 us
  starting transfers between devices: 7.01 us -> 7.85 us
    ppermute x0 -> x7, waiting for transfers between devices: none -> 22 us  [launch_the_screen(): jax.lax.ppermute(series[-1], axis_name=link_axis, perm=[(m, (m + 1) % tot...]
    all_gather x1 -> x0, blocking collectives: 9.32 us -> none  [body(): region_wake = lax.all_gather(wake_rows, 'narrow', axis=1, tiled=True)]
    ppermute x3, waiting for transfers between devices: 0.01 us -> 1.36 us  [exchange_slots(): by_shift.append(lax.ppermute(sent, 'region', pairs))]
    ppermute x0 -> x7, starting transfers between devices: none -> 1.26 us  [launch_the_screen(): jax.lax.ppermute(series[-1], axis_name=link_axis, perm=[(m, (m + 1) % tot...]
  transfers between devices with their start and end apart: 3 -> 10, of which waited for: 0 -> 7; matrix products, arithmetic and copies ran while one was open for 2% -> 3% of each run, Pallas kernels for 0% -> 0%
where the time goes in v1:
time: 48.9 us; the launch traced here: 48.5 us
  waiting for transfers between devices  23.4 us (48%)
  matrix products  10.2 us (21%)
  starting transfers between devices  7.85 us (16%)
  other arithmetic  3.92 us (8%)
  local copies, waits for them, and re-layouts  2.04 us (4%)
  between operations  0.94 us (2%)
    ppermute x7, waiting for transfers between devices, launch_the_screen(): jax.lax.ppermute(series[-1], axis_name=link_axis, perm=[(m, (m + 1) % tot...  22 us
    dot_general x4, matrix products, accumulate(): lax.dot_general(table_part, kernel, (((1,), (1,)), ((), ())), precision=l...  9.21 us
    ppermute x3, starting transfers between devices, exchange_slots(): by_shift.append(lax.ppermute(sent, 'region', pairs))  6.59 us
    ppermute x3, waiting for transfers between devices, exchange_slots(): by_shift.append(lax.ppermute(sent, 'region', pairs))  1.36 us
    ppermute x7, starting transfers between devices, launch_the_screen(): jax.lax.ppermute(series[-1], axis_name=link_axis, perm=[(m, (m + 1) % tot...  1.26 us
    dot_general x1, matrix products, body(): jnp.dot(dust_state, placing, precision=lax.Precision.HIGHEST, preferred_e...  1 us
  transfers between devices with their start and end apart: 10, of which 7 were waited for; matrix products, arithmetic and copies ran while one was open for 3% of the time, Pallas kernels for 0%

profile of v1, /device:TPU:0, one launch (start us, length us, event | category | flops | bytes accessed | tf_op | source)
XLA Modules:
  0.0 48.5 jit_solution(3729931973681833967)
XLA Ops:
  0.0 0.9 %convert_reduce_fusion = s32[192]{0:T(256)S(1)} fusion(s32[192]{0:T(256)} %bitcast.62), kind=kLoop, calls=%fused_computation.34 | loop fusion | flops 184128 | bytes 1536 | tf_op jit(solution)/shard_map/reduce_sum | solution.py:124
  0.9 0.7 %multiply_add_fusion.1 = s32[192,1]{0,1:T(1,128)S(1)} fusion(s32[192,1]{0,1:T(1,128)S(1)} %bitcast.65, s32[192,1]{0,1:T(1,128)} %param.16), kind=kLoop, calls=%fused_computation.107 | loop fusion | flops 384 | bytes 2304 | tf_op jit(solution)/shard_map/add | solution.py:125
  2.4 0.8 %pad_maximum_fusion = f32[7,1024]{1,0:T(8,128)S(1)} fusion(f32[1,1024]{1,0:T(1,128)} %bitcast.63, f32[3,1024]{1,0:T(4,128)} %param.19, f32[3,1024]{1,0:T(4,128)} %param.18), kind=kLoop, calls=%fused_computation.40 | loop fusion | flops 14336 | bytes 57344 | tf_op jit(solution)/shard_map/concatenate | solution.py:138
  3.1 1.0 %fusion.22 = f32[8,384]{1,0:T(8,128)S(1)} fusion(s32[192]{0:T(256)S(1)} %bitcast.69, f32[1,192]{1,0:T(1,128)} %bitcast.70, f32[3,192]{1,0:T(4,128)} %param.14, f32[3,192]{1,0:T(4,128)} %param.13, f32[8]{0:T(128)S(1)} %pad.21.clone, f32[192]{0:T(256)S(1)} %compare_convert_fusion), kind=kOutput, calls=%fused_computation.32 | convolution fusion | flops 7157760 | bytes 19232 | tf_op jit(solution)/shard_map/dot_general | solution.py:135
  4.1 0.5 collective-permute-start.3
  4.7 2.7 %collective-permute-start = (f32[8,96]{1,0:T(8,128)S(1)}, f32[8,96]{1,0:T(8,128)S(1)}, u32[]{:S(2)}, u32[]{:S(2)}) collective-permute-start(f32[8,96]{1,0:T(8,128)S(1)} %select_bitcast_fusion.2), channel_id=1, source_target_pairs={{0,8},{8,16},{16,24},{24,0},{1,9},{9,17},{17,25},{25,1},{2,10},{10... | collective-permute-start | bytes 9224 | tf_op jit(solution)/shard_map/ppermute | solution.py:109
  7.4 2.6 %collective-permute-start.1 = (f32[8,96]{1,0:T(8,128)S(1)}, f32[8,96]{1,0:T(8,128)S(1)}, u32[]{:S(2)}, u32[]{:S(2)}) collective-permute-start(f32[8,96]{1,0:T(8,128)S(1)} %select_bitcast_fusion.1), channel_id=1, source_target_pairs={{0,16},{8,24},{16,0},{24,8},{1,17},{9,25},{17,1},{25,9},{2,18},{10... | collective-permute-start | bytes 9224 | tf_op jit(solution)/shard_map/ppermute | solution.py:109
  10.0 1.3 %collective-permute-start.2 = (f32[8,96]{1,0:T(8,128)S(1)}, f32[8,96]{1,0:T(8,128)S(1)}, u32[]{:S(2)}, u32[]{:S(2)}) collective-permute-start(f32[8,96]{1,0:T(8,128)S(1)} %bitcast.64), channel_id=1, source_target_pairs={{0,24},{8,0},{16,8},{24,16},{1,25},{9,1},{17,9},{25,17},{2,26},{10... | collective-permute-start | bytes 9224 | tf_op jit(solution)/shard_map/ppermute | solution.py:109
  11.4 0.8 %collective-permute-start.4 = (f32[7,1024]{1,0:T(8,128)S(1)}, f32[7,1024]{1,0:T(8,128)S(1)}, u32[]{:S(2)}, u32[]{:S(2)}) collective-permute-start(f32[7,1024]{1,0:T(8,128)S(1)} %collective-permute-done.3), channel_id=1, source_target_pairs={{0,1},{1,2},{2,3},{3,4},{4,5},{5,6},{6,7},{7,0},{8,9},{9,10},{10,1... | collective-permute-start | bytes 86024 | tf_op jit(solution)/shard_map/ppermute | solution.py:16
  12.2 1.4 %collective-permute-done.2 = f32[8,96]{1,0:T(8,128)S(1)} collective-permute-done((f32[8,96]{1,0:T(8,128)S(1)}, f32[8,96]{1,0:T(8,128)S(1)}, u32[]{:S(2)}, u32[]{:S(2)}) %collective-permute-start.2) | collective-permute-done | bytes 3104 | tf_op jit(solution)/shard_map/ppermute | solution.py:109
  13.6 0.5 %gather_fusion = f32[4,8,96]{2,1,0:T(8,128)S(1)} fusion(f32[8,4,96]{2,0,1:T(8,128)S(1)} %pad_maximum_fusion.1, s32[1024]{0:T(1024)S(1)} %pad_clamp_fusion), kind=kCustom, calls=%fused_computation | custom fusion | bytes 24592 | tf_op jit(solution)/shard_map/jit(_take)/gather | solution.py:112
  14.1 1.6 %collective-permute-done.4 = f32[7,1024]{1,0:T(8,128)S(1)} collective-permute-done((f32[7,1024]{1,0:T(8,128)S(1)}, f32[7,1024]{1,0:T(8,128)S(1)}, u32[]{:S(2)}, u32[]{:S(2)}) %collective-permute-start.4) | collective-permute-done | bytes 28704 | tf_op jit(solution)/shard_map/ppermute | solution.py:16
  15.8 4.2 %collective-permute-done.5 = f32[7,1024]{1,0:T(8,128)S(1)} collective-permute-done((f32[7,1024]{1,0:T(8,128)S(1)}, f32[7,1024]{1,0:T(8,128)S(1)}, u32[]{:S(2)}, u32[]{:S(2)}) %collective-permute-start.5) | collective-permute-done | bytes 28704 | tf_op jit(solution)/shard_map/ppermute | solution.py:16
  20.0 4.2 %collective-permute-done.6 = f32[7,1024]{1,0:T(8,128)S(1)} collective-permute-done((f32[7,1024]{1,0:T(8,128)S(1)}, f32[7,1024]{1,0:T(8,128)S(1)}, u32[]{:S(2)}, u32[]{:S(2)}) %collective-permute-start.6) | collective-permute-done | bytes 28704 | tf_op jit(solution)/shard_map/ppermute | solution.py:16
  24.2 0.1 squeeze.30
  24.4 4.0 %collective-permute-done.7 = f32[7,1024]{1,0:T(8,128)S(1)} collective-permute-done((f32[7,1024]{1,0:T(8,128)S(1)}, f32[7,1024]{1,0:T(8,128)S(1)}, u32[]{:S(2)}, u32[]{:S(2)}) %collective-permute-start.7) | collective-permute-done | bytes 28704 | tf_op jit(solution)/shard_map/ppermute | solution.py:16
  28.4 4.2 %collective-permute-done.8 = f32[7,1024]{1,0:T(8,128)S(1)} collective-permute-done((f32[7,1024]{1,0:T(8,128)S(1)}, f32[7,1024]{1,0:T(8,128)S(1)}, u32[]{:S(2)}, u32[]{:S(2)}) %collective-permute-start.8) | collective-permute-done | bytes 28704 | tf_op jit(solution)/shard_map/ppermute | solution.py:16
  32.7 0.1 slice.122
  33.0 0.1 slice.124
  33.1 3.8 %collective-permute-done.9 = f32[7,1024]{1,0:T(8,128)S(1)} collective-permute-done((f32[7,1024]{1,0:T(8,128)S(1)}, f32[7,1024]{1,0:T(8,128)S(1)}, u32[]{:S(2)}, u32[]{:S(2)}) %collective-permute-start.9) | collective-permute-done | bytes 28704 | tf_op jit(solution)/shard_map/ppermute | solution.py:16
  37.1 0.1 constant_dynamic-slice_fusion.4
  37.2 0.5 %fusion.25 = (f32[8192]{0:T(1024)S(1)}, f32[1,8192]{1,0:T(1,128)S(1)}, f32[1,8192]{1,0:T(1,128)S(1)}, f32[1,8192]{1,0:T(1,128)S(1)}) fusion(f32[7,16384]{1,0:T(8,128)S(1)} %constant_dynamic-update-slice_fusion, s32[]{:T(128)S(6)} %add.167, s32[]{:T(128)S(6)} %select_n.90, s32[]{:T(128)S(6)} %add.165, s32[]{:T(128)S(6)} %add.164, s32[]{:T(128)S(6)} %add.163, ...), kind=kLoop, calls=%fused_computation.39 | loop fusion | flops 81920 | bytes 360476 | tf_op jit(solution)/shard_map/mul | solution.py:46
  37.8 0.1 maximum_bitcast_fusion
  37.9 9.8 %while.19 = (s32[]{:T(128)}, f32[6,384]{1,0:T(8,128)S(1)}, f32[4,6,2048]{2,1,0:T(8,128)S(1)}, f32[3,384]{1,0:T(4,128)S(1)}, f32[4,3,2048]{2,1,0:T(4,128)S(1)}, /...) while((s32[]{:T(128)}, f32[6,384]{1,0:T(8,128)S(1)}, ...), condition=%wide.region_2.4_spmd.clone, body=%wide.region_1.0_spmd.clone.sunk | while | flops 36966916 | bytes 200859 | solution.py:73
  38.0 2.3 %fusion.46 = f32[6,384]{1,0:T(8,128)S(1)} fusion(f32[2048]{0:T(1024)S(1)} %bitcast.55, f32[2048]{0:T(1024)S(1)} %bitcast.54, f32[384]{0:T(512)S(1)} %get-tuple-element.179, f32[2048]{0:T(1024)S(1)} %bitcast.53, f32[384]{0:T(512)S(1)} %get-tuple-element.181, f32[2048]{0:T(1024)S(1)} %bitcast.52, f32[384]{0:T(512)S(1)} %get-tuple-element.183, ...), kind=kOutput, calls=%fused_computation.20.clone.1 | convolution fusion | flops 36966912 | bytes 125957 | tf_op jit(solution)/shard_map/while/body/eval_jaxpr/while/body/eval_jaxpr/dot_general | solution.py:68
  40.3 0.1 constant_dynamic-slice_fusion.11
  40.5 2.3 %fusion.46 = f32[6,384]{1,0:T(8,128)S(1)} fusion(f32[2048]{0:T(1024)S(1)} %bitcast.55, f32[2048]{0:T(1024)S(1)} %bitcast.54, f32[384]{0:T(512)S(1)} %get-tuple-element.179, f32[2048]{0:T(1024)S(1)} %bitcast.53, f32[384]{0:T(512)S(1)} %get-tuple-element.181, f32[2048]{0:T(1024)S(1)} %bitcast.52, f32[384]{0:T(512)S(1)} %get-tuple-element.183, ...), kind=kOutput, calls=%fused_computation.20.clone.1 | convolution fusion | flops 36966912 | bytes 125957 | tf_op jit(solution)/shard_map/while/body/eval_jaxpr/while/body/eval_jaxpr/dot_general | solution.py:68
  42.8 0.1 constant_dynamic-slice_fusion.11
  42.9 2.3 %fusion.46 = f32[6,384]{1,0:T(8,128)S(1)} fusion(f32[2048]{0:T(1024)S(1)} %bitcast.55, f32[2048]{0:T(1024)S(1)} %bitcast.54, f32[384]{0:T(512)S(1)} %get-tuple-element.179, f32[2048]{0:T(1024)S(1)} %bitcast.53, f32[384]{0:T(512)S(1)} %get-tuple-element.181, f32[2048]{0:T(1024)S(1)} %bitcast.52, f32[384]{0:T(512)S(1)} %get-tuple-element.183, ...), kind=kOutput, calls=%fused_computation.20.clone.1 | convolution fusion | flops 36966912 | bytes 125957 | tf_op jit(solution)/shard_map/while/body/eval_jaxpr/while/body/eval_jaxpr/dot_general | solution.py:68
  45.2 0.1 constant_dynamic-slice_fusion.11
  45.4 2.3 %fusion.46 = f32[6,384]{1,0:T(8,128)S(1)} fusion(f32[2048]{0:T(1024)S(1)} %bitcast.55, f32[2048]{0:T(1024)S(1)} %bitcast.54, f32[384]{0:T(512)S(1)} %get-tuple-element.179, f32[2048]{0:T(1024)S(1)} %bitcast.53, f32[384]{0:T(512)S(1)} %get-tuple-element.181, f32[2048]{0:T(1024)S(1)} %bitcast.52, f32[384]{0:T(512)S(1)} %get-tuple-element.183, ...), kind=kOutput, calls=%fused_computation.20.clone.1 | convolution fusion | flops 36966912 | bytes 125957 | tf_op jit(solution)/shard_map/while/body/eval_jaxpr/while/body/eval_jaxpr/dot_general | solution.py:68
  47.8 0.6 %maximum_multiply_fusion = f32[6,384]{1,0:T(8,128)} fusion(f32[3,384]{1,0:T(4,128)S(1)} %get-tuple-element.114, f32[3,384]{1,0:T(4,128)S(1)} %get-tuple-element.113, f32[384]{0:T(512)S(1)} %squeeze.30), kind=kLoop, calls=%fused_computation.62 | loop fusion | flops 4608 | bytes 19968 | tf_op jit(solution)/shard_map/mul | solution.py:96
  (61 shorter events, 1.2 us)
Async XLA Ops:
  4.1 7.3 %collective-permute-start.3 = (f32[7,1024]{1,0:T(8,128)S(1)}, f32[7,1024]{1,0:T(8,128)S(1)}, u32[]{:S(2)}, u32[]{:S(2)}) collective-permute-start(f32[7,1024]{1,0:T(8,128)S(1)} %pad_maximum_fusion), channel_id=1, source_target_pairs={{0,1},{1,2},{2,3},{3,4},{4,5},{5,6},{6,7},{7,0},{8,9},{9,10},{10,1... | collective-permute-start | bytes 86024 | tf_op jit(solution)/shard_map/ppermute | solution.py:16
  4.7 7.5 %collective-permute-start = (f32[8,96]{1,0:T(8,128)S(1)}, f32[8,96]{1,0:T(8,128)S(1)}, u32[]{:S(2)}, u32[]{:S(2)}) collective-permute-start(f32[8,96]{1,0:T(8,128)S(1)} %select_bitcast_fusion.2), channel_id=1, source_target_pairs={{0,8},{8,16},{16,24},{24,0},{1,9},{9,17},{17,25},{25,1},{2,10},{10... | collective-permute-start | bytes 9224 | tf_op jit(solution)/shard_map/ppermute | solution.py:109
  7.4 4.8 %collective-permute-start.1 = (f32[8,96]{1,0:T(8,128)S(1)}, f32[8,96]{1,0:T(8,128)S(1)}, u32[]{:S(2)}, u32[]{:S(2)}) collective-permute-start(f32[8,96]{1,0:T(8,128)S(1)} %select_bitcast_fusion.1), channel_id=1, source_target_pairs={{0,16},{8,24},{16,0},{24,8},{1,17},{9,25},{17,1},{25,9},{2,18},{10... | collective-permute-start | bytes 9224 | tf_op jit(solution)/shard_map/ppermute | solution.py:109
  10.0 3.6 %collective-permute-start.2 = (f32[8,96]{1,0:T(8,128)S(1)}, f32[8,96]{1,0:T(8,128)S(1)}, u32[]{:S(2)}, u32[]{:S(2)}) collective-permute-start(f32[8,96]{1,0:T(8,128)S(1)} %bitcast.64), channel_id=1, source_target_pairs={{0,24},{8,0},{16,8},{24,16},{1,25},{9,1},{17,9},{25,17},{2,26},{10... | collective-permute-start | bytes 9224 | tf_op jit(solution)/shard_map/ppermute | solution.py:109
  11.4 4.3 %collective-permute-start.4 = (f32[7,1024]{1,0:T(8,128)S(1)}, f32[7,1024]{1,0:T(8,128)S(1)}, u32[]{:S(2)}, u32[]{:S(2)}) collective-permute-start(f32[7,1024]{1,0:T(8,128)S(1)} %collective-permute-done.3), channel_id=1, source_target_pairs={{0,1},{1,2},{2,3},{3,4},{4,5},{5,6},{6,7},{7,0},{8,9},{9,10},{10,1... | collective-permute-start | bytes 86024 | tf_op jit(solution)/shard_map/ppermute | solution.py:16
  15.7 4.2 %collective-permute-start.5 = (f32[7,1024]{1,0:T(8,128)S(1)}, f32[7,1024]{1,0:T(8,128)S(1)}, u32[]{:S(2)}, u32[]{:S(2)}) collective-permute-start(f32[7,1024]{1,0:T(8,128)S(1)} %collective-permute-done.4), channel_id=1, source_target_pairs={{0,1},{1,2},{2,3},{3,4},{4,5},{5,6},{6,7},{7,0},{8,9},{9,10},{10,1... | collective-permute-start | bytes 86024 | tf_op jit(solution)/shard_map/ppermute | solution.py:16
  19.9 4.2 %collective-permute-start.6 = (f32[7,1024]{1,0:T(8,128)S(1)}, f32[7,1024]{1,0:T(8,128)S(1)}, u32[]{:S(2)}, u32[]{:S(2)}) collective-permute-start(f32[7,1024]{1,0:T(8,128)S(1)} %collective-permute-done.5), channel_id=1, source_target_pairs={{0,1},{1,2},{2,3},{3,4},{4,5},{5,6},{6,7},{7,0},{8,9},{9,10},{10,1... | collective-permute-start | bytes 86024 | tf_op jit(solution)/shard_map/ppermute | solution.py:16
  24.2 4.2 %collective-permute-start.7 = (f32[7,1024]{1,0:T(8,128)S(1)}, f32[7,1024]{1,0:T(8,128)S(1)}, u32[]{:S(2)}, u32[]{:S(2)}) collective-permute-start(f32[7,1024]{1,0:T(8,128)S(1)} %collective-permute-done.6), channel_id=1, source_target_pairs={{0,1},{1,2},{2,3},{3,4},{4,5},{5,6},{6,7},{7,0},{8,9},{9,10},{10,1... | collective-permute-start | bytes 86024 | tf_op jit(solution)/shard_map/ppermute | solution.py:16
  28.4 4.2 %collective-permute-start.8 = (f32[7,1024]{1,0:T(8,128)S(1)}, f32[7,1024]{1,0:T(8,128)S(1)}, u32[]{:S(2)}, u32[]{:S(2)}) collective-permute-start(f32[7,1024]{1,0:T(8,128)S(1)} %collective-permute-done.7), channel_id=1, source_target_pairs={{0,1},{1,2},{2,3},{3,4},{4,5},{5,6},{6,7},{7,0},{8,9},{9,10},{10,1... | collective-permute-start | bytes 86024 | tf_op jit(solution)/shard_map/ppermute | solution.py:16
  32.7 4.2 %collective-permute-start.9 = (f32[7,1024]{1,0:T(8,128)S(1)}, f32[7,1024]{1,0:T(8,128)S(1)}, u32[]{:S(2)}, u32[]{:S(2)}) collective-permute-start(f32[7,1024]{1,0:T(8,128)S(1)} %collective-permute-done.8), channel_id=1, source_target_pairs={{0,1},{1,2},{2,3},{3,4},{4,5},{5,6},{6,7},{7,0},{8,9},{9,10},{10,1... | collective-permute-start | bytes 86024 | tf_op jit(solution)/shard_map/ppermute | solution.py:16
  37.9 9.9 %copy-start = (f32[3]{0:T(128)S(1)}, f32[3]{0:T(128)}, u32[]{:S(2)}) copy-start(f32[3]{0:T(128)} %constant.155) | copy-start | bytes 40
